TPU v7x, 256 devices: a whole 4x4x8 slice. The times are simulated.
256 devices in a mesh: dp: 16 (over z, core), group: 16 (over x, y).
Axes of the slice: x: 4, y: 4, z: 8, core: 2. Of those that a mesh axis runs over, the one named last changes fastest.
Arguments:
- hidden_in: bfloat16 [16, 16, 128, 5120], P('dp', 'group'), may hold values from -48 to 48
- gain: float32 [5120], replicated, may hold values from 0.1 to 1.9
- value_weight: bfloat16 [5120, 512], P(('dp', 'group')), may hold values from -0.078125 to 0.078125
- value_cot: bfloat16 [16, 16, 128, 512], P('dp', 'group'), may hold values from -6 to 6
- lengths: int32 [16, 16], P('dp', 'group'), may hold values from 1 to 128, as said below
- rewards: int32 [16, 16], P('dp', 'group'), may hold values from 0 to 3
Outputs:
- values: bfloat16 [16, 16, 128, 512], P('dp', 'group')
- weight_grad: float32 [5120, 512], P(('dp', 'group'))
- gain_grad: float32 [5120], P(('dp', 'group'))
Inputs may be any that keep to these rules, and one draw needn't show every extreme that they name: `lengths`: some response has exactly 128 tokens.
All inputs are finite; a program needn't handle non-finite values.
Results may differ from a plain program's by a relative error of at most 0.019.
Values may be sent and summed in bfloat16 or wider, within the bound.
No kernel may reach another device: no remote copies, remote signals or barrier semaphores. Data moves between devices by JAX's collectives and lax.ppermute only.
A program may use at most 64 MiB of HBM per device.

v0:
```python
import jax
import jax.numpy as jnp
from jax import lax
from jax.sharding import PartitionSpec as P


def body(hidden_in, gain, value_weight, value_cot, lengths, rewards):
    prompts, answers, length, features = hidden_in.shape
    kv_width = value_weight.shape[1]
    row_count = prompts * answers * length
    n_dp = lax.axis_size("dp")
    n_group = lax.axis_size("group")
    group_count = answers * n_group
    shard_rows = value_weight.shape[0]
    scores = rewards.astype(jnp.float32)
    peer_scores = lax.all_to_all(
        jnp.broadcast_to(scores.reshape(1, -1), (n_group, scores.size)), "group", 0, 0, tiled=True
    )
    reward_sum = jnp.sum(peer_scores).reshape(1, 1)
    square_sum = jnp.sum(peer_scores * peer_scores).reshape(1, 1)
    centre = reward_sum / group_count
    spread = square_sum / group_count - centre * centre
    advantage = (scores - centre) / jnp.maximum(jnp.sqrt(spread), 1.0)
    position = jnp.arange(length)
    alive_mask = position[None, None, :] < lengths[:, :, None]
    token_weight = jnp.where(alive_mask, (advantage / lengths.astype(jnp.float32))[:, :, None], 0.0)
    flat_in = hidden_in.reshape(row_count, features)
    inverse = lax.rsqrt(
        jnp.mean(jnp.square(flat_in.astype(jnp.float32)), axis=1, keepdims=True) + 1e-06
    )
    normed = (flat_in.astype(jnp.float32) * inverse * gain).astype(jnp.bfloat16)
    scaled_cot = (
        token_weight.reshape(row_count, 1)
        * value_cot.reshape(row_count, kv_width).astype(jnp.float32)
    ).astype(jnp.bfloat16)
    part = lax.all_to_all(
        jnp.broadcast_to(value_weight[None], (n_group,) + value_weight.shape),
        "group",
        0,
        0,
        tiled=True,
    ).reshape(n_group * shard_rows, kv_width)
    full_weight = lax.all_gather(part, "dp", axis=0, tiled=True)
    projected = jnp.dot(normed, full_weight, preferred_element_type=jnp.float32)
    back = lax.dot_general(
        scaled_cot, full_weight, (((1,), (1,)), ((), ())), preferred_element_type=jnp.float32
    )
    gain_term = jnp.sum(back * (flat_in.astype(jnp.float32) * inverse), axis=0)
    values = projected.astype(jnp.bfloat16).reshape(prompts, answers, length, kv_width)
    grad_part = lax.dot_general(
        normed, scaled_cot, (((0,), (0,)), ((), ())), preferred_element_type=jnp.float32
    )
    grad_part = lax.psum_scatter(
        grad_part.reshape(n_dp, features // n_dp, kv_width).astype(jnp.bfloat16),
        "dp",
        scatter_dimension=0,
        tiled=True,
    )
    grad_part = grad_part.astype(jnp.float32).reshape(n_group, shard_rows, kv_width)
    weight_grad = lax.all_to_all(grad_part, "group", 0, 0, tiled=True).sum(0)
    gain_part = lax.all_to_all(gain_term.reshape(n_dp, features // n_dp), "dp", 0, 0, tiled=True)
    gain_part = gain_part.sum(0).reshape(n_group, shard_rows)
    gain_grad = lax.all_to_all(gain_part, "group", 0, 0, tiled=True).sum(0)
    return (values, weight_grad, gain_grad)


def solution(mesh):
    in_specs = (
        P("dp", "group", None, None),
        P(),
        P(("dp", "group"), None),
        P("dp", "group", None, None),
        P("dp", "group"),
        P("dp", "group"),
    )
    out_specs = (P("dp", "group", None, None), P(("dp", "group"), None), P(("dp", "group")))
    return jax.shard_map(body, mesh=mesh, in_specs=in_specs, out_specs=out_specs, check_vma=False)
```

profile of v0, /device:TPU:8, one launch (start us, length us, event | category | flops | bytes accessed | tf_op | source)
XLA Modules:
  0.0 162.0 jit_solution(6888291572416146831)
XLA Ops:
  7.2 0.0 copy-start
  7.2 0.0 copy-start.2
  7.2 0.0 all-gather.2.cloned.1.call-start
  7.2 0.9 broadcast_in_dim.32
  8.1 15.4 %all_to_all.34 = bf16[16,20,512]{2,1,0:T(8,128)(2,1)S(1)} all-to-all(bf16[16,20,512]{2,1,0:T(8,128)(2,1)S(1)} %broadcast_in_dim.32), channel_id=1, replica_groups=mesh['dp'=16,'group'=16] {'group'}, dimensions={0} | all-to-all | bytes 655360 | tf_op jit(solution)/shard_map/all_to_all | solution.py:36
  23.5 0.8 reshape.96
  24.3 0.0 all-gather.2.cloned.1.call-update
  24.9 0.6 broadcast_in_dim.34
  25.5 5.3 %all-to-all-start.1 = ((f32[16,1,1]{2,1,0:T(1,128)}), f32[16,1,1]{2,1,0:T(1,128)S(1)}, u32[]{:S(2)}, u32[]{:S(2)}) async-start(f32[16,1,1]{2,1,0:T(1,128)} %broadcast_in_dim.34), calls=%async_computation.1 | async-start | bytes 16384 | tf_op jit(solution)/shard_map/all_to_all | solution.py:16
  30.9 0.0 reduce-scatter.2.cloned.1.call-start
  31.6 0.0 copy-done
  31.6 0.3 fusion.2
  31.9 5.1 %all-to-all-done.1 = f32[16,1,1]{2,1,0:T(1,128)S(1)} async-done(((f32[16,1,1]{2,1,0:T(1,128)}), f32[16,1,1]{2,1,0:T(1,128)S(1)}, u32[]{:S(2)}, u32[]{:S(2)}) %all-to-all-start.1) | async-done | bytes 96 | tf_op jit(solution)/shard_map/all_to_all | solution.py:16
  37.0 0.6 reduce_sum.64
  39.6 0.1 copy.18
  39.7 0.6 multiply_reduce_fusion
  41.0 0.0 copy-done.2
  41.1 0.0 copy-start.1
  41.1 0.4 fusion.5
  41.5 1.4 copy.17
  42.9 0.0 copy-done.1
  42.9 5.3 %convolution_convert_fusion = bf16[16,320,512]{2,1,0:T(8,128)(2,1)} fusion(bf16[16,320,128]{2,1,0:T(8,128)(2,1)} %bitcast.35, bf16[1,1,128,512]{3,2,1,0:T(8,128)(2,1)S(1)} %copy-done.1, f32[128]{0:T(128)S(1)} %get-tuple-element.3), kind=kOutput, calls=%fused_computation.4 | convolution fusion | flops 673906688 | bytes 6685184 | tf_op jit(solution)/shard_map/dot_general | solution.py:50
  48.2 0.0 reduce-scatter.2.cloned.1.call-update
  48.2 20.3 %all-gather.2.cloned.1.call-done = bf16[5120,512]{1,0:T(8,128)(2,1)} async-done(((bf16[320,512]{1,0:T(8,128)(2,1)}), bf16[5120,512]{1,0:T(8,128)(2,1)}) %all-gather.2.cloned.1.call-update) | async-done | bytes 5242896 | tf_op jit(solution)/shard_map/all_gather | solution.py:43
  68.5 4.3 %fusion.3 = f32[5120]{0:T(1024)S(1)} fusion(bf16[5120,512]{1,0:T(8,128)(2,1)} %all-gather.2.cloned.1.call-done, bf16[1,1,128,5120]{3,2,1,0:T(8,128)(2,1)S(1)} %copy-done, f32[128]{0:T(128)S(1)} %get-tuple-element.4, bf16[1,1,128,512]{3,2,1,0:T(8,128)(2,1)S(1)} %copy-done.1, f32[128]{0:T(128)S(1)} %get-tuple-element.3), kind=kOutput, calls=%fused_computation.7 | convolution fusion | flops 673901568 | bytes 6706176 | tf_op jit(solution)/shard_map/dot_general | solution.py:45
  72.8 0.1 all_to_all.25
  72.9 11.9 %all_to_all.35 = f32[16,1,320]{2,1,0:T(1,128)S(1)} all-to-all(f32[16,1,320]{2,1,0:T(1,128)S(1)} %all_to_all.25), channel_id=1, replica_groups=mesh['dp'=16,'group'=16] {'dp'}, dimensions={0} | all-to-all | bytes 40960 | tf_op jit(solution)/shard_map/all_to_all | solution.py:61
  84.8 0.7 all_to_all.27
  85.5 7.4 %all-to-all-start.4 = ((f32[16,1,20]{2,1,0:T(1,128)}), f32[16,1,20]{2,1,0:T(1,128)S(1)}, u32[]{:S(2)}, u32[]{:S(2)}) async-start(f32[16,1,20]{2,1,0:T(1,128)} %all_to_all.27), calls=%async_computation.5 | async-start | bytes 16384 | tf_op jit(solution)/shard_map/all_to_all | solution.py:63
  92.9 42.3 %reduce-scatter.2.cloned.1.call-done = bf16[1,320,512]{2,1,0:T(8,128)(2,1)} async-done(((bf16[16,320,512]{2,1,0:T(8,128)(2,1)}), bf16[1,320,512]{2,1,0:T(8,128)(2,1)}) %reduce-scatter.2.cloned.1.call-update) | async-done | bytes 327696 | tf_op jit(solution)/shard_map/reduce_scatter | solution.py:53
  135.2 1.9 %reshape.104 = f32[16,20,512]{2,1,0:T(8,128)} reshape(bf16[1,320,512]{2,1,0:T(8,128)(2,1)} %reduce-scatter.2.cloned.1.call-done) | data formatting | bytes 983040 | tf_op jit(solution)/shard_map/reshape | solution.py:59
  137.2 0.0 all-to-all-done.4
  137.2 7.1 %all-to-all-start.2 = ((f32[16,20,512]{2,1,0:T(8,128)}), f32[16,20,512]{2,1,0:T(8,128)S(1)}, u32[]{:S(2)}, u32[]{:S(2)}) async-start(f32[16,20,512]{2,1,0:T(8,128)} %reshape.104), calls=%async_computation.3 | async-start | bytes 1572864 | tf_op jit(solution)/shard_map/all_to_all | solution.py:60
  144.3 4.0 %fusion.4 = bf16[1,1,128,512]{3,2,1,0:T(8,128)(2,1)} fusion(bf16[5120,512]{1,0:T(8,128)(2,1)} %all-gather.2.cloned.1.call-done, bf16[1,1,128,5120]{3,2,1,0:T(8,128)(2,1)S(1)} %copy-done, f32[5120]{0:T(1024)S(1)} %copy-done.2, f32[128]{0:T(128)S(1)} %get-tuple-element.4), kind=kOutput, calls=%fused_computation.9 | convolution fusion | flops 673775616 | bytes 6705664 | tf_op jit(solution)/shard_map/dot_general | solution.py:44
  148.3 0.5 reduce_sum.69
  148.9 5.6 %all-to-all-done.2 = f32[16,20,512]{2,1,0:T(8,128)S(1)} async-done(((f32[16,20,512]{2,1,0:T(8,128)}), f32[16,20,512]{2,1,0:T(8,128)S(1)}, u32[]{:S(2)}, u32[]{:S(2)}) %all-to-all-start.2) | async-done | bytes 655392 | tf_op jit(solution)/shard_map/all_to_all | solution.py:60
  154.4 0.7 reduce_sum.66
  (2 shorter events, 0.0 us)
Async XLA Ops:
  7.2 24.4 %copy-start = (bf16[1,1,128,5120]{3,2,1,0:T(8,128)(2,1)S(1)}, bf16[1,1,128,5120]{3,2,1,0:T(8,128)(2,1)}, u32[]{:S(2)}) copy-start(bf16[1,1,128,5120]{3,2,1,0:T(8,128)(2,1)} %param.6) | copy-start | bytes 3932164
  7.2 33.9 %copy-start.2 = (f32[5120]{0:T(1024)S(1)}, f32[5120]{0:T(1024)}, u32[]{:S(2)}) copy-start(f32[5120]{0:T(1024)} %param.7) | copy-start | bytes 61444
  7.2 61.3 %all-gather.2.cloned.1.call-start = ((), (), s32[]{:S(2)}) async-start(), calls=%async_computation.6 | async-start | bytes 5570560 | tf_op jit(solution)/shard_map/all_gather | solution.py:43
  25.5 11.5 %all-to-all-start.1 = ((f32[16,1,1]{2,1,0:T(1,128)}), f32[16,1,1]{2,1,0:T(1,128)S(1)}, u32[]{:S(2)}, u32[]{:S(2)}) async-start(f32[16,1,1]{2,1,0:T(1,128)} %broadcast_in_dim.34), calls=%async_computation.1 | async-start | bytes 16384 | tf_op jit(solution)/shard_map/all_to_all | solution.py:16
  30.9 104.4 %reduce-scatter.2.cloned.1.call-start = ((), (), s32[]{:S(2)}) async-start(), calls=%async_computation.7 | async-start | bytes 5570560 | tf_op jit(solution)/shard_map/reduce_scatter | solution.py:53
  41.1 1.8 %copy-start.1 = (bf16[1,1,128,512]{3,2,1,0:T(8,128)(2,1)S(1)}, bf16[1,1,128,512]{3,2,1,0:T(8,128)(2,1)}, u32[]{:S(2)}) copy-start(bf16[1,1,128,512]{3,2,1,0:T(8,128)(2,1)} %param.9) | copy-start | bytes 393220
  85.5 51.7 %all-to-all-start.4 = ((f32[16,1,20]{2,1,0:T(1,128)}), f32[16,1,20]{2,1,0:T(1,128)S(1)}, u32[]{:S(2)}, u32[]{:S(2)}) async-start(f32[16,1,20]{2,1,0:T(1,128)} %all_to_all.27), calls=%async_computation.5 | async-start | bytes 16384 | tf_op jit(solution)/shard_map/all_to_all | solution.py:63
  137.2 17.3 %all-to-all-start.2 = ((f32[16,20,512]{2,1,0:T(8,128)}), f32[16,20,512]{2,1,0:T(8,128)S(1)}, u32[]{:S(2)}, u32[]{:S(2)}) async-start(f32[16,20,512]{2,1,0:T(8,128)} %reshape.104), calls=%async_computation.3 | async-start | bytes 1572864 | tf_op jit(solution)/shard_map/all_to_all | solution.py:60
Sparse Core Ops, SparseCore 0:
  24.4 44.0 all-gather.1
  71.1 64.1 reduce-scatter.1
where the time goes:
time: 163 us; the launch traced here: 162 us
  waiting for transfers between devices  73.3 us (45%)
  blocking collectives  27.2 us (17%)
  starting transfers between devices  19.9 us (12%)
  between operations  18.1 us (11%)
  matrix products  13.6 us (8%)
  local copies, waits for them, and re-layouts  6.51 us (4%)
  other arithmetic  3.2 us (2%)
    reduce_scatter x1, waiting for transfers between devices, body(): lax.psum_scatter(grad_part.reshape(n_dp, features // n_dp, kv_width).asty...  42.3 us
    all_gather x1, waiting for transfers between devices, body(): full_weight = lax.all_gather(part, 'dp', axis=0, tiled=True)  20.3 us
    all_to_all x1, blocking collectives, body(): lax.all_to_all(jnp.broadcast_to(value_weight[None], (n_group,) + value_we...  15.4 us
    all_to_all x1, blocking collectives, body(): lax.all_to_all(gain_term.reshape(n_dp, features // n_dp), 'dp', 0, 0, til...  11.9 us
    all_to_all x1, starting transfers between devices, body(): gain_grad = lax.all_to_all(gain_part, 'group', 0, 0, tiled=True).sum(0)  7.4 us
    all_to_all x1, starting transfers between devices, body(): weight_grad = lax.all_to_all(grad_part, 'group', 0, 0, tiled=True).sum(0)  7.12 us
    all_to_all x1, waiting for transfers between devices, body(): weight_grad = lax.all_to_all(grad_part, 'group', 0, 0, tiled=True).sum(0)  5.57 us
    all_to_all x1, starting transfers between devices, body(): lax.all_to_all(jnp.broadcast_to(scores.reshape(1, -1), (n_group, scores.s...  5.35 us
  transfers between devices with their start and end apart: 5, of which 4 were waited for; matrix products, arithmetic and copies ran while one was open for 12% of the time, Pallas kernels for 0%

commit v1 on v0

--- a/solution.py
+++ b/solution.py
@@ -40,7 +40,14 @@
         0,
         tiled=True,
     ).reshape(n_group * shard_rows, kv_width)
-    full_weight = lax.all_gather(part, "dp", axis=0, tiled=True)
+
+    def supply_all_waves_for(bus_axis, arr_in):
+        all_blocks = []
+        for _ in range(lax.axis_size(bus_axis)):
+            all_blocks.append(arr_in)
+        return jnp.concatenate(lax.all_to_all(jnp.stack(all_blocks), bus_axis, 0, 0), axis=0)
+
+    full_weight = supply_all_waves_for("dp", part)
     projected = jnp.dot(normed, full_weight, preferred_element_type=jnp.float32)
     back = lax.dot_general(
         scaled_cot, full_weight, (((1,), (1,)), ((), ())), preferred_element_type=jnp.float32

time: 163 us -> 247 us (1.52)
  blocking collectives: 27.2 us -> 162 us
  waiting for transfers between devices: 73.3 us -> 15.7 us
  starting transfers between devices: 19.9 us -> 24.4 us
  local copies, waits for them, and re-layouts: 6.51 us -> 9.29 us
  matrix products: 13.6 us -> 11.1 us
    all_to_all x1, blocking collectives: 15.4 us -> 150 us  [supply_all_waves_for(): lax.all_to_all(jnp.stack(all_blocks), bus_axis, 0, 0)]
    reduce_scatter x1, waiting for transfers between devices: 42.3 us -> 0.01 us  [body(): lax.psum_scatter(grad_part.reshape(n_dp, features // n_dp, kv_width).asty...]
    all_gather x1 -> x0, waiting for transfers between devices: 20.3 us -> none  [body(): full_weight = lax.all_gather(part, 'dp', axis=0, tiled=True)]
    all_to_all x0 -> x1, starting transfers between devices: none -> 4.8 us  [body(): lax.all_to_all(jnp.broadcast_to(value_weight[None], (n_group,) + value_we...]
    all_to_all x1, waiting for transfers between devices: 0.01 us -> 4.22 us  [body(): gain_grad = lax.all_to_all(gain_part, 'group', 0, 0, tiled=True).sum(0)]
  transfers between devices with their start and end apart: 5 -> 5, of which waited for: 4 -> 3; matrix products, arithmetic and copies ran while one was open for 12% -> 8% of each run, Pallas kernels for 0% -> 0%
where the time goes in v1:
time: 247 us; the launch traced here: 246 us
  blocking collectives  162 us (66%)
  starting transfers between devices  24.4 us (10%)
  between operations  18.2 us (7%)
  waiting for transfers between devices  15.7 us (6%)
  matrix products  11.1 us (4%)
  local copies, waits for them, and re-layouts  9.29 us (4%)
  other arithmetic  5.28 us (2%)
    all_to_all x1, blocking collectives, supply_all_waves_for(): lax.all_to_all(jnp.stack(all_blocks), bus_axis, 0, 0)  150 us
    all_to_all x1, blocking collectives, body(): lax.all_to_all(gain_term.reshape(n_dp, features // n_dp), 'dp', 0, 0, til...  12.3 us
    all_to_all x1, waiting for transfers between devices, body(): weight_grad = lax.all_to_all(grad_part, 'group', 0, 0, tiled=True).sum(0)  7.57 us
    all_to_all x1, starting transfers between devices, body(): lax.all_to_all(jnp.broadcast_to(scores.reshape(1, -1), (n_group, scores.s...  7.39 us
    all_to_all x1, starting transfers between devices, body(): gain_grad = lax.all_to_all(gain_part, 'group', 0, 0, tiled=True).sum(0)  7.28 us
    dot_general x1, matrix products, body(): lax.dot_general(normed, scaled_cot, (((0,), (0,)), ((), ())), preferred_e...  5.21 us
  transfers between devices with their start and end apart: 5, of which 3 were waited for; matrix products, arithmetic and copies ran while one was open for 8% of the time, Pallas kernels for 0%

profile of v1, /device:TPU:8, one launch (start us, length us, event | category | flops | bytes accessed | tf_op | source)
XLA Modules:
  0.0 246.3 jit_solution(10689861893098363771)
XLA Ops:
  7.2 0.0 copy-start.1
  7.9 0.6 broadcast_in_dim.34
  8.5 7.4 %all-to-all-start.2 = ((f32[16,1,1]{2,1,0:T(1,128)}), f32[16,1,1]{2,1,0:T(1,128)S(1)}, u32[]{:S(2)}, u32[]{:S(2)}) async-start(f32[16,1,1]{2,1,0:T(1,128)} %broadcast_in_dim.34), calls=%async_computation.2 | async-start | bytes 16384 | tf_op jit(solution)/shard_map/all_to_all | solution.py:16
  16.6 1.7 fusion.4
  18.2 3.8 %all-to-all-done.2 = f32[16,1,1]{2,1,0:T(1,128)S(1)} async-done(((f32[16,1,1]{2,1,0:T(1,128)}), f32[16,1,1]{2,1,0:T(1,128)S(1)}, u32[]{:S(2)}, u32[]{:S(2)}) %all-to-all-start.2) | async-done | bytes 96 | tf_op jit(solution)/shard_map/all_to_all | solution.py:16
  22.1 1.5 broadcast_in_dim.32
  23.6 4.8 %all-to-all-start = ((bf16[16,20,512]{2,1,0:T(8,128)(2,1)}), bf16[16,20,512]{2,1,0:T(8,128)(2,1)S(1)}, u32[]{:S(2)}, u32[]{:S(2)}) async-start(bf16[16,20,512]{2,1,0:T(8,128)(2,1)} %broadcast_in_dim.32), calls=%async_computation | async-start | bytes 786432 | tf_op jit(solution)/shard_map/all_to_all | solution.py:36
  28.4 0.0 reduce-scatter.2.cloned.1.call-start
  28.4 0.6 reduce_sum.64
  31.0 0.1 copy.18
  31.1 0.6 multiply_reduce_fusion
  32.5 0.0 copy-done.1
  32.5 0.0 copy-start.2
  32.5 1.1 fusion.11
  33.6 1.5 copy.17
  35.1 0.0 copy-done.2
  35.1 5.2 %convolution_convert_fusion = bf16[16,320,512]{2,1,0:T(8,128)(2,1)} fusion(bf16[16,320,128]{2,1,0:T(8,128)(2,1)} %bitcast.50, bf16[1,1,128,512]{3,2,1,0:T(8,128)(2,1)S(1)} %copy-done.2, f32[128]{0:T(128)S(1)} %get-tuple-element.3), kind=kOutput, calls=%fused_computation.6 | convolution fusion | flops 673906688 | bytes 6685184 | tf_op jit(solution)/shard_map/dot_general | solution.py:57
  40.3 0.0 reduce-scatter.2.cloned.1.call-update
  40.3 0.0 all-to-all-done
  40.3 0.1 stack_reshape.2
  40.4 0.5 stack.3
  40.9 150.0 %all_to_all.39 = bf16[16,320,512]{2,1,0:T(8,128)(2,1)S(1)} all-to-all(bf16[16,320,512]{2,1,0:T(8,128)(2,1)S(1)} %stack.3), channel_id=1, replica_groups=mesh['dp'=16,'group'=16] {'dp'}, dimensions={0} | all-to-all | bytes 10485760 | tf_op jit(solution)/shard_map/all_to_all | solution.py:48
  191.0 0.0 copy-start
  191.0 2.3 copy-done
  193.3 1.9 fusion.7
  195.2 0.0 copy-start.3
  195.2 0.1 all_to_all.29
  195.3 12.3 %all_to_all.40 = f32[16,1,320]{2,1,0:T(1,128)S(1)} all-to-all(f32[16,1,320]{2,1,0:T(1,128)S(1)} %all_to_all.29), channel_id=1, replica_groups=mesh['dp'=16,'group'=16] {'dp'}, dimensions={0} | all-to-all | bytes 40960 | tf_op jit(solution)/shard_map/all_to_all | solution.py:68
  207.6 0.7 all_to_all.31
  208.3 7.3 %all-to-all-start.5 = ((f32[16,1,20]{2,1,0:T(1,128)}), f32[16,1,20]{2,1,0:T(1,128)S(1)}, u32[]{:S(2)}, u32[]{:S(2)}) async-start(f32[16,1,20]{2,1,0:T(1,128)} %all_to_all.31), calls=%async_computation.6 | async-start | bytes 16384 | tf_op jit(solution)/shard_map/all_to_all | solution.py:70
  215.6 0.0 reduce-scatter.2.cloned.1.call-done
  215.6 1.9 reshape.126
  217.5 4.2 %all-to-all-done.5 = f32[16,1,20]{2,1,0:T(1,128)S(1)} async-done(((f32[16,1,20]{2,1,0:T(1,128)}), f32[16,1,20]{2,1,0:T(1,128)S(1)}, u32[]{:S(2)}, u32[]{:S(2)}) %all-to-all-start.5) | async-done | bytes 1312 | tf_op jit(solution)/shard_map/all_to_all | solution.py:70
  221.8 4.9 %all-to-all-start.3 = ((f32[16,20,512]{2,1,0:T(8,128)}), f32[16,20,512]{2,1,0:T(8,128)S(1)}, u32[]{:S(2)}, u32[]{:S(2)}) async-start(f32[16,20,512]{2,1,0:T(8,128)} %reshape.126), calls=%async_computation.4 | async-start | bytes 1572864 | tf_op jit(solution)/shard_map/all_to_all | solution.py:67
  226.6 0.0 copy-done.3
  226.6 4.0 %fusion.17 = bf16[1,1,128,512]{3,2,1,0:T(8,128)(2,1)} fusion(bf16[5120,512]{1,0:T(8,128)(2,1)} %bitcast.49, bf16[1,1,128,5120]{3,2,1,0:T(8,128)(2,1)S(1)} %copy-done.1, f32[5120]{0:T(1024)S(1)} %copy-done.3, f32[128]{0:T(128)S(1)} %get-tuple-element.4), kind=kOutput, calls=%fused_computation.18 | convolution fusion | flops 673775616 | bytes 6705664 | tf_op jit(solution)/shard_map/dot_general | solution.py:51
  230.7 0.5 reduce_sum.69
  231.2 7.6 %all-to-all-done.3 = f32[16,20,512]{2,1,0:T(8,128)S(1)} async-done(((f32[16,20,512]{2,1,0:T(8,128)}), f32[16,20,512]{2,1,0:T(8,128)S(1)}, u32[]{:S(2)}, u32[]{:S(2)}) %all-to-all-start.3) | async-done | bytes 655392 | tf_op jit(solution)/shard_map/all_to_all | solution.py:67
  238.8 0.7 reduce_sum.66
  (2 shorter events, 0.0 us)
Async XLA Ops:
  7.2 25.3 %copy-start.1 = (bf16[1,1,128,5120]{3,2,1,0:T(8,128)(2,1)S(1)}, bf16[1,1,128,5120]{3,2,1,0:T(8,128)(2,1)}, u32[]{:S(2)}) copy-start(bf16[1,1,128,5120]{3,2,1,0:T(8,128)(2,1)} %param.6) | copy-start | bytes 3932164
  8.5 13.5 %all-to-all-start.2 = ((f32[16,1,1]{2,1,0:T(1,128)}), f32[16,1,1]{2,1,0:T(1,128)S(1)}, u32[]{:S(2)}, u32[]{:S(2)}) async-start(f32[16,1,1]{2,1,0:T(1,128)} %broadcast_in_dim.34), calls=%async_computation.2 | async-start | bytes 16384 | tf_op jit(solution)/shard_map/all_to_all | solution.py:16
  23.6 16.7 %all-to-all-start = ((bf16[16,20,512]{2,1,0:T(8,128)(2,1)}), bf16[16,20,512]{2,1,0:T(8,128)(2,1)S(1)}, u32[]{:S(2)}, u32[]{:S(2)}) async-start(bf16[16,20,512]{2,1,0:T(8,128)(2,1)} %broadcast_in_dim.32), calls=%async_computation | async-start | bytes 786432 | tf_op jit(solution)/shard_map/all_to_all | solution.py:36
  28.4 187.2 %reduce-scatter.2.cloned.1.call-start = ((), (), s32[]{:S(2)}) async-start(), calls=%async_computation.7 | async-start | bytes 5570560 | tf_op jit(solution)/shard_map/reduce_scatter | solution.py:60
  32.5 2.6 %copy-start.2 = (bf16[1,1,128,512]{3,2,1,0:T(8,128)(2,1)S(1)}, bf16[1,1,128,512]{3,2,1,0:T(8,128)(2,1)}, u32[]{:S(2)}) copy-start(bf16[1,1,128,512]{3,2,1,0:T(8,128)(2,1)} %param.9) | copy-start | bytes 393220
  191.0 2.3 copy-start
  195.2 31.4 %copy-start.3 = (f32[5120]{0:T(1024)S(1)}, f32[5120]{0:T(1024)}, u32[]{:S(2)}) copy-start(f32[5120]{0:T(1024)} %param.7) | copy-start | bytes 61444
  208.3 13.4 %all-to-all-start.5 = ((f32[16,1,20]{2,1,0:T(1,128)}), f32[16,1,20]{2,1,0:T(1,128)S(1)}, u32[]{:S(2)}, u32[]{:S(2)}) async-start(f32[16,1,20]{2,1,0:T(1,128)} %all_to_all.31), calls=%async_computation.6 | async-start | bytes 16384 | tf_op jit(solution)/shard_map/all_to_all | solution.py:70
  221.8 17.0 %all-to-all-start.3 = ((f32[16,20,512]{2,1,0:T(8,128)}), f32[16,20,512]{2,1,0:T(8,128)S(1)}, u32[]{:S(2)}, u32[]{:S(2)}) async-start(f32[16,20,512]{2,1,0:T(8,128)} %reshape.126), calls=%async_computation.4 | async-start | bytes 1572864 | tf_op jit(solution)/shard_map/all_to_all | solution.py:67
Sparse Core Ops, SparseCore 0:
  40.4 153.9 reduce-scatter.1
